TPU v7x, 128 devices: a whole 4x4x4 slice. The times are simulated.
128 devices in a mesh: enc: 16 (over z, y), dp: 2 (over x_hi), tensor: 4 (over x_lo, core).
Axes of the slice: x: 4 (x_hi: 2, x_lo: 2; x = x_hi * 2 + x_lo), y: 4, z: 4, core: 2. Of those that a mesh axis runs over, the one named last changes fastest.
Arguments:
- hidden_in: bfloat16 [3, 64, 4096], P(None, 'dp', 'enc')
- self_cache: bfloat16 [64, 8, 2, 2048], P(('dp', 'enc'), None, None, 'tensor'), may hold values from -6 to 6
- src_pool: bfloat16 [64, 24, 2, 2048], P(('dp', 'enc'), None, None, 'tensor'), may hold values from -6 to 6
- assign: int32 [64], replicated, may hold values from 0 to 63, as said below
- src_len: int32 [64], replicated, may hold values from 1 to 24, 768 in all
- positions: int32 [64], replicated, may hold values from 1 to 8, 256 in all
- gain_self: float32 [4096], P('enc'), may hold values from 0.1 to 1.9
- w_qkv: bfloat16 [4096, 3, 2048], P('enc', None, 'tensor'), may hold values from -0.09375 to 0.09375
- w_out_self: bfloat16 [2048, 4096], P('tensor', 'enc'), may hold values from -0.125 to 0.125
- gain_cross: float32 [4096], P('enc'), may hold values from 0.1 to 1.9
- w_q_cross: bfloat16 [4096, 2048], P('enc', 'tensor'), may hold values from -0.09375 to 0.09375
- w_out_cross: bfloat16 [2048, 4096], P('tensor', 'enc'), may hold values from -0.125 to 0.125
Outputs:
- layer_out: bfloat16 [3, 64, 4096], P(None, 'dp', 'enc')
Inputs may be any that keep to these rules, and one draw needn't show every extreme that they name: `assign`: a permutation of the 64 sources; with blocks of 2 consecutive sequences or sources numbered d * 16 + e, the 2 sequences of block d * 16 + e read exactly one source from each block d2 * 16 + e that has the same e.
All inputs are finite; a program needn't handle non-finite values.
Results may differ from a plain program's by a relative error of at most 0.008.
Values may be sent and summed in bfloat16 or wider, within the bound.
No kernel may reach another device: no remote copies, remote signals or barrier semaphores. Data moves between devices by JAX's collectives and lax.ppermute only.
A program may use at most 64 MiB of HBM per device.

v0:
```python
import math
import jax
import jax.numpy as jnp
from jax import lax
from jax.sharding import PartitionSpec as P

D = 4096
DK = 256
STEPS = 3
EPSILON = 1e-06


def row_norm(rows_in, gain_vec):
    squares = lax.psum(jnp.sum(rows_in * rows_in, axis=1), "enc")
    return (rows_in * lax.rsqrt(squares / D + EPSILON)[:, None] * gain_vec[None, :]).astype(
        jnp.bfloat16
    )


def score_weight(scores):
    return jnp.exp(scores).astype(jnp.bfloat16)


def attend(query_rows, key_rows, value_rows, usable):
    count = query_rows.shape[0]
    head_count = query_rows.shape[1] // DK
    query_heads = query_rows.reshape(count, head_count, DK)
    key_heads = key_rows.reshape(count, key_rows.shape[1], head_count, DK)
    value_heads = value_rows.reshape(count, value_rows.shape[1], head_count, DK)
    scores = jnp.einsum(
        "nhd,nlhd->nhl", query_heads, key_heads, preferred_element_type=jnp.float32
    ) * (1.0 / math.sqrt(DK))
    weights = jnp.where(usable[:, None, :], score_weight(scores), jnp.zeros((), jnp.bfloat16))
    weighted = jnp.einsum("nhl,nlhd->nhd", weights, value_heads, preferred_element_type=jnp.float32)
    return (weighted, jnp.sum(weights.astype(jnp.float32), axis=-1))


def combine_heads(context, weight_out):
    partial_out = jnp.dot(context, weight_out, preferred_element_type=jnp.float32)
    return lax.psum(partial_out, "tensor")


def on_device(
    hidden_in,
    self_cache,
    src_pool,
    assign,
    src_len,
    positions,
    gain_self,
    w_qkv,
    w_out_self,
    gain_cross,
    w_q_cross,
    w_out_cross,
):
    dp_count = lax.axis_size("dp")
    enc_count = lax.axis_size("enc")
    seq_dev = self_cache.shape[0]
    per_pair = seq_dev // dp_count
    cache_len = self_cache.shape[1]
    source_len = src_pool.shape[1]
    enc_at = lax.axis_index("enc")
    dp_at = lax.axis_index("dp")
    block_at = dp_at * enc_count + enc_at
    slot_index = jnp.arange(seq_dev, dtype=jnp.int32)
    my_slots = block_at * seq_dev + slot_index
    my_positions = jnp.take(positions, my_slots)
    my_sources = jnp.take(assign, my_slots)
    place_at = jnp.arange(cache_len, dtype=jnp.int32)
    cache_usable = place_at[None, :] < my_positions[:, None]
    token_at = jnp.arange(source_len, dtype=jnp.int32)
    assign_view = assign.reshape(dp_count, enc_count, seq_dev)
    assign_grid = jnp.take(assign_view, enc_at, axis=1)
    owners = assign_grid // (seq_dev * enc_count)
    earlier = (owners[:, None, :] == owners[:, :, None]) & (
        slot_index[None, None, :] < slot_index[None, :, None]
    )
    slot_rank = jnp.sum(earlier.astype(jnp.int32), axis=2)
    recv_rows = jnp.take(owners, dp_at, axis=0) * per_pair + jnp.take(slot_rank, dp_at, axis=0)
    picked = (owners == dp_at)[:, :, None] & (
        slot_rank[:, :, None] == jnp.arange(per_pair, dtype=jnp.int32)[None, None, :]
    )
    chosen = jnp.sum(jnp.where(picked, (assign_grid % seq_dev)[:, :, None], 0), axis=1)
    chosen_flat = chosen.reshape(-1)
    outgoing = jnp.take(src_pool, chosen_flat, axis=0)
    arrived = lax.all_to_all(outgoing, "dp", split_axis=0, concat_axis=0, tiled=True)
    cross_kv = jnp.take(arrived, recv_rows, axis=0)
    cross_usable = token_at[None, :] < jnp.take(src_len, my_sources)[:, None]
    key_list = []
    value_list = []
    results = []
    for step_at in range(STEPS):
        current = hidden_in[step_at].astype(jnp.float32)
        normed = row_norm(current, gain_self)
        projected = jnp.einsum("sd,dcw->scw", normed, w_qkv, preferred_element_type=jnp.float32)
        own_proj = lax.psum_scatter(projected, "enc", scatter_dimension=0, tiled=True).astype(
            jnp.bfloat16
        )
        query_rows = own_proj[:, 0]
        key_list.append(own_proj[:, 1])
        value_list.append(own_proj[:, 2])
        weighted, totals = attend(
            query_rows, self_cache[:, :, 0], self_cache[:, :, 1], cache_usable
        )
        head_count = weighted.shape[1]
        query_heads = query_rows.astype(jnp.float32).reshape(seq_dev, head_count, DK)
        for key_new, value_new in zip(key_list, value_list):
            scores = jnp.sum(
                query_heads * key_new.astype(jnp.float32).reshape(seq_dev, head_count, DK), axis=-1
            ) * (1.0 / math.sqrt(DK))
            weights = score_weight(scores).astype(jnp.float32)
            weighted = weighted + weights[:, :, None] * value_new.astype(jnp.float32).reshape(
                seq_dev, head_count, DK
            )
            totals = totals + weights
        context = (
            (weighted / totals[:, :, None]).reshape(seq_dev, head_count * DK).astype(jnp.bfloat16)
        )
        context_all = lax.all_gather(context, "enc", axis=0, tiled=True)
        residual = current + combine_heads(context_all, w_out_self)
        normed_cross = row_norm(residual, gain_cross)
        cross_query = jnp.dot(normed_cross, w_q_cross, preferred_element_type=jnp.float32)
        own_query = lax.psum_scatter(cross_query, "enc", scatter_dimension=0, tiled=True).astype(
            jnp.bfloat16
        )
        weighted, totals = attend(own_query, cross_kv[:, :, 0], cross_kv[:, :, 1], cross_usable)
        context = (
            (weighted / totals[:, :, None]).reshape(seq_dev, head_count * DK).astype(jnp.bfloat16)
        )
        context_all = lax.all_gather(context, "enc", axis=0, tiled=True)
        output_rows = residual + combine_heads(context_all, w_out_cross)
        results.append(output_rows.astype(jnp.bfloat16))
    return jnp.stack(results)


def solution(mesh):
    in_specs = (
        P(None, "dp", "enc"),
        P(("dp", "enc"), None, None, "tensor"),
        P(("dp", "enc"), None, None, "tensor"),
        P(),
        P(),
        P(),
        P("enc"),
        P("enc", None, "tensor"),
        P("tensor", "enc"),
        P("enc"),
        P("enc", "tensor"),
        P("tensor", "enc"),
    )
    out_specs = P(None, "dp", "enc")
    return jax.shard_map(
        on_device, mesh=mesh, in_specs=in_specs, out_specs=out_specs, check_vma=False
    )
```

profile of v0, /device:TPU:1, one launch (start us, length us, event | category | flops | bytes accessed | tf_op | source)
XLA Modules:
  0.0 470.3 jit_solution(5215867503166297110)
XLA Ops:
  8.7 0.7 gather_fusion.3
  9.4 0.8 broadcast_select_fusion.1
  10.2 5.0 %all-to-all-start = ((bf16[2,24,2,512]{3,2,1,0:T(2,128)(2,1)}), bf16[2,24,2,512]{3,2,1,0:T(2,128)(2,1)S(1)}, u32[]{:S(2)}, u32[]{:S(2)}) async-start(bf16[2,24,2,512]{3,2,1,0:T(2,128)(2,1)} %broadcast_select_fusion.1), calls=%async_computation | async-start | bytes 196608 | tf_op jit(solution)/shard_map/all_to_all | solution.py:87
  15.3 34.7 %all-reduce.9 = (f32[32]{0:T(128)S(1)}, f32[32]{0:T(128)S(1)}, f32[32]{0:T(128)S(1)}) all-reduce(f32[32]{0:T(128)S(1)} %get-tuple-element.35, f32[32]{0:T(128)S(1)} %get-tuple-element.36, f32[32]{0:T(128)S(1)} %get-tuple-element.37), channel_id=1, replica_groups=mesh['enc'=16,'dp'=2,'tensor'=4] {'enc'}, use_global_device_ids=true, to_apply=%region_1.3 | all-reduce | flops 96 | bytes 768 | tf_op jit(solution)/shard_map/psum | solution.py:14
  53.5 62.2 %all-reduce.20 = (bf16[32,3,512]{2,0,1:T(8,128)(2,1)S(1)}, bf16[32,3,512]{2,0,1:T(8,128)(2,1)S(1)}, bf16[32,3,512]{2,0,1:T(8,128)(2,1)S(1)}) all-reduce(f32[32,3,512]{2,0,1:T(8,128)S(1)} %fusion.40, f32[32,3,512]{2,0,1:T(8,128)S(1)} %fusion.34, f32[32,3,512]{2,0,1:T(8,128)S(1)} %fusion.37), channel_id=2, replica_groups=mesh['enc'=16,'dp'=2,'tensor'=4] {'enc'}, use_global_device_ids=true, to_apply=%region_2.4.clone | all-reduce | flops 147456 | bytes 884736
  119.0 15.2 %all-gather = bf16[16,2,512]{2,1,0:T(2,128)(2,1)S(1)} all-gather(bf16[1,2,512]{2,1,0:T(2,128)(2,1)S(1)} %reshape.380), channel_id=1, replica_groups=mesh['enc'=16,'dp'=2,'tensor'=4] {'enc'}, dimensions={0}, use_global_device_ids=true | all-gather | bytes 34816 | tf_op jit(solution)/shard_map/all_gather | solution.py:120
  134.2 18.0 %all-gather.2 = bf16[16,2,512]{2,1,0:T(2,128)(2,1)S(1)} all-gather(bf16[1,2,512]{2,1,0:T(2,128)(2,1)S(1)} %reshape.384), channel_id=1, replica_groups=mesh['enc'=16,'dp'=2,'tensor'=4] {'enc'}, dimensions={0}, use_global_device_ids=true | all-gather | bytes 34816 | tf_op jit(solution)/shard_map/all_gather | solution.py:120
  152.3 0.8 fusion.102
  153.1 0.8 fusion.105
  153.8 15.4 %all-gather.4 = bf16[16,2,512]{2,1,0:T(2,128)(2,1)S(1)} all-gather(bf16[1,2,512]{2,1,0:T(2,128)(2,1)S(1)} %reshape.388), channel_id=1, replica_groups=mesh['enc'=16,'dp'=2,'tensor'=4] {'enc'}, dimensions={0}, use_global_device_ids=true | all-gather | bytes 34816 | tf_op jit(solution)/shard_map/all_gather | solution.py:120
  169.3 0.8 fusion.108
  171.4 0.7 gather_fusion.4
  172.8 70.9 %all-reduce.19.cloned.1.call-done = (f32[32,256]{1,0:T(8,128)}, f32[32,256]{1,0:T(8,128)}, f32[32,256]{1,0:T(8,128)}) async-done(((f32[32,256]{1,0:T(8,128)}, f32[32,256]{1,0:T(8,128)}, f32[32,256]{1,0:T(8,128)}), (f32[32,256]{1,0:T(8,128)}, f32[32,256]{1,0:T(8,128)}, f32[32,256]{1,0:T(8,128)})) %all-reduce.19.cloned.1.call-update) | async-done | bytes 98320 | tf_op jit(solution)/shard_map/psum | solution.py:40
  243.7 1.0 multiply_reduce_fusion.2
  244.6 33.3 %all-reduce.7 = (f32[32]{0:T(128)S(1)}, f32[32]{0:T(128)S(1)}, f32[32]{0:T(128)S(1)}) all-reduce(f32[32]{0:T(128)S(1)} %get-tuple-element.34, f32[32]{0:T(128)S(1)} %get-tuple-element.33, f32[32]{0:T(128)S(1)} %get-tuple-element.32), channel_id=1, replica_groups=mesh['enc'=16,'dp'=2,'tensor'=4] {'enc'}, use_global_device_ids=true, to_apply=%region_34.38 | all-reduce | flops 96 | bytes 768 | tf_op jit(solution)/shard_map/psum | solution.py:14
  280.4 57.3 %all-reduce.21 = (bf16[32,512]{1,0:T(8,128)(2,1)S(1)}, bf16[32,512]{1,0:T(8,128)(2,1)S(1)}, bf16[32,512]{1,0:T(8,128)(2,1)S(1)}) all-reduce(f32[32,512]{1,0:T(8,128)S(1)} %fusion.31, f32[32,512]{1,0:T(8,128)S(1)} %fusion.29, f32[32,512]{1,0:T(8,128)S(1)} %fusion.27), channel_id=7, replica_groups=mesh['enc'=16,'dp'=2,'tensor'=4] {'enc'}, use_global_device_ids=true, to_apply=%region_35.39.clone | all-reduce | flops 49152 | bytes 294912
  338.5 16.3 %all-gather.1 = bf16[16,2,512]{2,1,0:T(2,128)(2,1)S(1)} all-gather(bf16[1,2,512]{2,1,0:T(2,128)(2,1)S(1)} %reshape.382), channel_id=1, replica_groups=mesh['enc'=16,'dp'=2,'tensor'=4] {'enc'}, dimensions={0}, use_global_device_ids=true | all-gather | bytes 34816 | tf_op jit(solution)/shard_map/all_gather | solution.py:131
  355.0 17.4 %all-gather.3 = bf16[16,2,512]{2,1,0:T(2,128)(2,1)S(1)} all-gather(bf16[1,2,512]{2,1,0:T(2,128)(2,1)S(1)} %reshape.386), channel_id=1, replica_groups=mesh['enc'=16,'dp'=2,'tensor'=4] {'enc'}, dimensions={0}, use_global_device_ids=true | all-gather | bytes 34816 | tf_op jit(solution)/shard_map/all_gather | solution.py:131
  372.5 0.8 fusion.103
  373.2 0.8 fusion.106
  374.2 15.7 %all-gather.5 = bf16[16,2,512]{2,1,0:T(2,128)(2,1)S(1)} all-gather(bf16[1,2,512]{2,1,0:T(2,128)(2,1)S(1)} %reshape.390), channel_id=1, replica_groups=mesh['enc'=16,'dp'=2,'tensor'=4] {'enc'}, dimensions={0}, use_global_device_ids=true | all-gather | bytes 34816 | tf_op jit(solution)/shard_map/all_gather | solution.py:131
  389.9 0.8 fusion.109
  390.7 71.3 %all-reduce.17.cloned.1.call-done = (f32[32,256]{1,0:T(8,128)}, f32[32,256]{1,0:T(8,128)}, f32[32,256]{1,0:T(8,128)}) async-done(((f32[32,256]{1,0:T(8,128)}, f32[32,256]{1,0:T(8,128)}, f32[32,256]{1,0:T(8,128)}), (f32[32,256]{1,0:T(8,128)}, f32[32,256]{1,0:T(8,128)}, f32[32,256]{1,0:T(8,128)})) %all-reduce.17.cloned.1.call-update) | async-done | bytes 98320 | tf_op jit(solution)/shard_map/psum | solution.py:40
  462.1 0.8 fusion.28
  (133 shorter events, 14.4 us)
Async XLA Ops:
  6.5 43.5 %copy-start = (bf16[256,3,512]{2,0,1:T(8,128)(2,1)S(1)}, bf16[256,3,512]{2,0,1:T(8,128)(2,1)}, u32[]{:S(2)}) copy-start(bf16[256,3,512]{2,0,1:T(8,128)(2,1)} %param.25) | copy-start | bytes 2359300
  6.6 0.7 copy-start.1
  7.8 0.9 copy-start.12
  10.2 5.0 %copy-start.7 = (bf16[3,32,256]{2,1,0:T(8,128)(2,1)S(1)}, bf16[3,32,256]{2,1,0:T(8,128)(2,1)}, u32[]{:S(2)}) copy-start(bf16[3,32,256]{2,1,0:T(8,128)(2,1)} %param.18) | copy-start | bytes 147460
  10.2 161.2 %all-to-all-start = ((bf16[2,24,2,512]{3,2,1,0:T(2,128)(2,1)}), bf16[2,24,2,512]{3,2,1,0:T(2,128)(2,1)S(1)}, u32[]{:S(2)}, u32[]{:S(2)}) async-start(bf16[2,24,2,512]{3,2,1,0:T(2,128)(2,1)} %broadcast_select_fusion.1), calls=%async_computation | async-start | bytes 196608 | tf_op jit(solution)/shard_map/all_to_all | solution.py:87
  15.2 228.5 %all-reduce.19.cloned.1.call-start = ((), (), s32[]{:S(2)}) async-start(), calls=%async_computation.2 | async-start | bytes 196608 | tf_op jit(solution)/shard_map/psum | solution.py:40
  50.0 0.7 copy-start.14
  51.6 0.7 copy-start.15
  115.8 0.8 copy-start.11
  116.9 0.7 copy-start.2
  118.2 34.1 %copy-start.4 = (bf16[512,256]{1,0:T(8,128)(2,1)S(1)}, bf16[512,256]{1,0:T(8,128)(2,1)}, u32[]{:S(2)}) copy-start(bf16[512,256]{1,0:T(8,128)(2,1)} %param.26) | copy-start | bytes 786436
  170.0 0.7 copy-start.3
  170.0 292.0 %all-reduce.17.cloned.1.call-start = ((), (), s32[]{:S(2)}) async-start(), calls=%async_computation.1 | async-start | bytes 196608 | tf_op jit(solution)/shard_map/psum | solution.py:40
  172.3 105.7 %copy-start.6 = (bf16[256,512]{1,0:T(8,128)(2,1)S(1)}, bf16[256,512]{1,0:T(8,128)(2,1)}, u32[]{:S(2)}) copy-start(bf16[256,512]{1,0:T(8,128)(2,1)} %param.28) | copy-start | bytes 786436
  243.7 34.4 %copy-start.8 = (f32[32,256]{1,0:T(8,128)S(1)}, f32[32,256]{1,0:T(8,128)}, u32[]{:S(2)}) copy-start(f32[32,256]{1,0:T(8,128)} %get-tuple-element.64) | copy-start | bytes 98308
  278.0 0.7 copy-start.13
  278.7 0.8 copy-start.9
  279.4 0.8 copy-start.10
  337.9 34.6 %copy-start.5 = (bf16[512,256]{1,0:T(8,128)(2,1)S(1)}, bf16[512,256]{1,0:T(8,128)(2,1)}, u32[]{:S(2)}) copy-start(bf16[512,256]{1,0:T(8,128)(2,1)} %param.29) | copy-start | bytes 786436
Sparse Core Ops, SparseCore 0:
  170.2 73.4 all-reduce.18
  390.8 71.1 all-reduce.16
where the time goes:
time: 471 us; the launch traced here: 470 us
  blocking collectives  286 us (61%)
  waiting for transfers between devices  142 us (30%)
  between operations  14.4 us (3%)
  local copies, waits for them, and re-layouts  10.8 us (2%)
  matrix products  7.41 us (2%)
  starting transfers between devices  5 us (1%)
  other arithmetic  4.79 us (1%)
    psum x2, waiting for transfers between devices, combine_heads(): return lax.psum(partial_out, 'tensor')  142 us
    unnamed x2, blocking collectives  120 us
    all_gather x6, blocking collectives, on_device(): context_all = lax.all_gather(context, 'enc', axis=0, tiled=True)  98 us
    psum x2, blocking collectives, row_norm(): squares = lax.psum(jnp.sum(rows_in * rows_in, axis=1), 'enc')  68.1 us
  transfers between devices with their start and end apart: 3, of which 2 were waited for; matrix products, arithmetic and copies ran while one was open for 2% of the time, Pallas kernels for 0%

commit v1 on v0

--- a/solution.py
+++ b/solution.py
@@ -128,7 +128,9 @@
         context = (
             (weighted / totals[:, :, None]).reshape(seq_dev, head_count * DK).astype(jnp.bfloat16)
         )
-        context_all = lax.all_gather(context, "enc", axis=0, tiled=True)
+        context_all = jnp.concatenate(
+            lax.all_to_all(jnp.stack([context] * lax.axis_size("enc")), "enc", 0, 0), axis=0
+        )
         output_rows = residual + combine_heads(context_all, w_out_cross)
         results.append(output_rows.astype(jnp.bfloat16))
     return jnp.stack(results)

time: 471 us -> 438 us (0.930)
  blocking collectives: 286 us -> 236 us
  starting transfers between devices: 5 us -> 15.5 us
    all_gather x6 -> x3, blocking collectives: 98 us -> 48.6 us  [on_device(): context_all = lax.all_gather(context, 'enc', axis=0, tiled=True)]
    all_to_all x0 -> x3, waiting for transfers between devices: none -> 17.1 us  [on_device(): lax.all_to_all(jnp.stack([context] * lax.axis_size('enc')), 'enc', 0, 0)]
    psum x2, waiting for transfers between devices: 142 us -> 129 us  [combine_heads(): return lax.psum(partial_out, 'tensor')]
    all_to_all x0 -> x3, starting transfers between devices: none -> 10.5 us  [on_device(): lax.all_to_all(jnp.stack([context] * lax.axis_size('enc')), 'enc', 0, 0)]
  transfers between devices with their start and end apart: 3 -> 6, of which waited for: 2 -> 5; matrix products, arithmetic and copies ran while one was open for 2% -> 2% of each run, Pallas kernels for 0% -> 0%
where the time goes in v1:
time: 438 us; the launch traced here: 437 us
  blocking collectives  236 us (54%)
  waiting for transfers between devices  146 us (33%)
  starting transfers between devices  15.5 us (4%)
  between operations  14.5 us (3%)
  local copies, waits for them, and re-layouts  12.7 us (3%)
  matrix products  7.41 us (2%)
  other arithmetic  4.79 us (1%)
    psum x2, waiting for transfers between devices, combine_heads(): return lax.psum(partial_out, 'tensor')  129 us
    unnamed x2, blocking collectives  120 us
    psum x2, blocking collectives, row_norm(): squares = lax.psum(jnp.sum(rows_in * rows_in, axis=1), 'enc')  68.1 us
    all_gather x3, blocking collectives, on_device(): context_all = lax.all_gather(context, 'enc', axis=0, tiled=True)  48.6 us
    all_to_all x3, waiting for transfers between devices, on_device(): lax.all_to_all(jnp.stack([context] * lax.axis_size('enc')), 'enc', 0, 0)  17.1 us
    all_to_all x3, starting transfers between devices, on_device(): lax.all_to_all(jnp.stack([context] * lax.axis_size('enc')), 'enc', 0, 0)  10.5 us
  transfers between devices with their start and end apart: 6, of which 5 were waited for; matrix products, arithmetic and copies ran while one was open for 2% of the time, Pallas kernels for 0%

profile of v1, /device:TPU:1, one launch (start us, length us, event | category | flops | bytes accessed | tf_op | source)
XLA Modules:
  0.0 437.0 jit_solution(14208301053967108881)
XLA Ops:
  9.4 0.8 broadcast_select_fusion.1
  10.2 5.0 %all-to-all-start = ((bf16[2,24,2,512]{3,2,1,0:T(2,128)(2,1)}), bf16[2,24,2,512]{3,2,1,0:T(2,128)(2,1)S(1)}, u32[]{:S(2)}, u32[]{:S(2)}) async-start(bf16[2,24,2,512]{3,2,1,0:T(2,128)(2,1)} %broadcast_select_fusion.1), calls=%async_computation | async-start | bytes 196608 | tf_op jit(solution)/shard_map/all_to_all | solution.py:87
  15.3 34.7 %all-reduce.9 = (f32[32]{0:T(128)S(1)}, f32[32]{0:T(128)S(1)}, f32[32]{0:T(128)S(1)}) all-reduce(f32[32]{0:T(128)S(1)} %get-tuple-element.35, f32[32]{0:T(128)S(1)} %get-tuple-element.36, f32[32]{0:T(128)S(1)} %get-tuple-element.37), channel_id=1, replica_groups=mesh['enc'=16,'dp'=2,'tensor'=4] {'enc'}, use_global_device_ids=true, to_apply=%region_1.3 | all-reduce | flops 96 | bytes 768 | tf_op jit(solution)/shard_map/psum | solution.py:14
  53.5 62.2 %all-reduce.20 = (bf16[32,3,512]{2,0,1:T(8,128)(2,1)S(1)}, bf16[32,3,512]{2,0,1:T(8,128)(2,1)S(1)}, bf16[32,3,512]{2,0,1:T(8,128)(2,1)S(1)}) all-reduce(f32[32,3,512]{2,0,1:T(8,128)S(1)} %fusion.40, f32[32,3,512]{2,0,1:T(8,128)S(1)} %fusion.34, f32[32,3,512]{2,0,1:T(8,128)S(1)} %fusion.37), channel_id=2, replica_groups=mesh['enc'=16,'dp'=2,'tensor'=4] {'enc'}, use_global_device_ids=true, to_apply=%region_2.4.clone | all-reduce | flops 147456 | bytes 884736
  119.0 15.2 %all-gather = bf16[16,2,512]{2,1,0:T(2,128)(2,1)S(1)} all-gather(bf16[1,2,512]{2,1,0:T(2,128)(2,1)S(1)} %reshape.401), channel_id=1, replica_groups=mesh['enc'=16,'dp'=2,'tensor'=4] {'enc'}, dimensions={0}, use_global_device_ids=true | all-gather | bytes 34816 | tf_op jit(solution)/shard_map/all_gather | solution.py:120
  134.2 18.0 %all-gather.1 = bf16[16,2,512]{2,1,0:T(2,128)(2,1)S(1)} all-gather(bf16[1,2,512]{2,1,0:T(2,128)(2,1)S(1)} %reshape.403), channel_id=1, replica_groups=mesh['enc'=16,'dp'=2,'tensor'=4] {'enc'}, dimensions={0}, use_global_device_ids=true | all-gather | bytes 34816 | tf_op jit(solution)/shard_map/all_gather | solution.py:120
  152.3 0.8 fusion.105
  153.1 0.8 fusion.108
  153.8 15.4 %all-gather.2 = bf16[16,2,512]{2,1,0:T(2,128)(2,1)S(1)} all-gather(bf16[1,2,512]{2,1,0:T(2,128)(2,1)S(1)} %reshape.405), channel_id=1, replica_groups=mesh['enc'=16,'dp'=2,'tensor'=4] {'enc'}, dimensions={0}, use_global_device_ids=true | all-gather | bytes 34816 | tf_op jit(solution)/shard_map/all_gather | solution.py:120
  169.3 0.8 fusion.111
  172.7 70.9 %all-reduce.19.cloned.1.call-done = (f32[32,256]{1,0:T(8,128)}, f32[32,256]{1,0:T(8,128)}, f32[32,256]{1,0:T(8,128)}) async-done(((f32[32,256]{1,0:T(8,128)}, f32[32,256]{1,0:T(8,128)}, f32[32,256]{1,0:T(8,128)}), (f32[32,256]{1,0:T(8,128)}, f32[32,256]{1,0:T(8,128)}, f32[32,256]{1,0:T(8,128)})) %all-reduce.19.cloned.1.call-update) | async-done | bytes 98320 | tf_op jit(solution)/shard_map/psum | solution.py:40
  243.7 1.0 multiply_reduce_fusion.2
  244.6 33.3 %all-reduce.7 = (f32[32]{0:T(128)S(1)}, f32[32]{0:T(128)S(1)}, f32[32]{0:T(128)S(1)}) all-reduce(f32[32]{0:T(128)S(1)} %get-tuple-element.34, f32[32]{0:T(128)S(1)} %get-tuple-element.33, f32[32]{0:T(128)S(1)} %get-tuple-element.32), channel_id=1, replica_groups=mesh['enc'=16,'dp'=2,'tensor'=4] {'enc'}, use_global_device_ids=true, to_apply=%region_34.38 | all-reduce | flops 96 | bytes 768 | tf_op jit(solution)/shard_map/psum | solution.py:14
  280.4 57.3 %all-reduce.21 = (bf16[32,512]{1,0:T(8,128)(2,1)S(1)}, bf16[32,512]{1,0:T(8,128)(2,1)S(1)}, bf16[32,512]{1,0:T(8,128)(2,1)S(1)}) all-reduce(f32[32,512]{1,0:T(8,128)S(1)} %fusion.31, f32[32,512]{1,0:T(8,128)S(1)} %fusion.29, f32[32,512]{1,0:T(8,128)S(1)} %fusion.27), channel_id=7, replica_groups=mesh['enc'=16,'dp'=2,'tensor'=4] {'enc'}, use_global_device_ids=true, to_apply=%region_35.39.clone | all-reduce | flops 49152 | bytes 294912
  339.1 3.5 all-to-all-start.1
  343.1 6.0 %all-to-all-done.1 = bf16[16,2,512]{2,1,0:T(2,128)(2,1)S(1)} async-done(((bf16[16,2,512]{2,1,0:T(2,128)(2,1)}), bf16[16,2,512]{2,1,0:T(2,128)(2,1)S(1)}, u32[]{:S(2)}, u32[]{:S(2)}) %all-to-all-start.1) | async-done | bytes 32800 | tf_op jit(solution)/shard_map/all_to_all | solution.py:132
  349.7 3.5 all-to-all-start.2
  354.0 5.6 %all-to-all-done.2 = bf16[16,2,512]{2,1,0:T(2,128)(2,1)S(1)} async-done(((bf16[16,2,512]{2,1,0:T(2,128)(2,1)}), bf16[16,2,512]{2,1,0:T(2,128)(2,1)S(1)}, u32[]{:S(2)}, u32[]{:S(2)}) %all-to-all-start.2) | async-done | bytes 32800 | tf_op jit(solution)/shard_map/all_to_all | solution.py:132
  360.2 3.5 all-to-all-start.3
  363.8 0.8 fusion.109
  364.5 5.6 %all-to-all-done.3 = bf16[16,2,512]{2,1,0:T(2,128)(2,1)S(1)} async-done(((bf16[16,2,512]{2,1,0:T(2,128)(2,1)}), bf16[16,2,512]{2,1,0:T(2,128)(2,1)S(1)}, u32[]{:S(2)}, u32[]{:S(2)}) %all-to-all-start.3) | async-done | bytes 32800 | tf_op jit(solution)/shard_map/all_to_all | solution.py:132
  370.1 0.8 fusion.112
  370.9 57.8 %all-reduce.17.cloned.1.call-done = (f32[32,256]{1,0:T(8,128)}, f32[32,256]{1,0:T(8,128)}, f32[32,256]{1,0:T(8,128)}) async-done(((f32[32,256]{1,0:T(8,128)}, f32[32,256]{1,0:T(8,128)}, f32[32,256]{1,0:T(8,128)}), (f32[32,256]{1,0:T(8,128)}, f32[32,256]{1,0:T(8,128)}, f32[32,256]{1,0:T(8,128)})) %all-reduce.17.cloned.1.call-update) | async-done | bytes 98320 | tf_op jit(solution)/shard_map/psum | solution.py:40
  428.7 0.8 fusion.28
  (139 shorter events, 18.6 us)
Async XLA Ops:
  6.5 43.5 %copy-start = (bf16[256,3,512]{2,0,1:T(8,128)(2,1)S(1)}, bf16[256,3,512]{2,0,1:T(8,128)(2,1)}, u32[]{:S(2)}) copy-start(bf16[256,3,512]{2,0,1:T(8,128)(2,1)} %param.25) | copy-start | bytes 2359300
  6.6 0.7 copy-start.1
  7.8 0.9 copy-start.12
  10.2 5.0 %copy-start.7 = (bf16[3,32,256]{2,1,0:T(8,128)(2,1)S(1)}, bf16[3,32,256]{2,1,0:T(8,128)(2,1)}, u32[]{:S(2)}) copy-start(bf16[3,32,256]{2,1,0:T(8,128)(2,1)} %param.18) | copy-start | bytes 147460
  10.2 161.2 %all-to-all-start = ((bf16[2,24,2,512]{3,2,1,0:T(2,128)(2,1)}), bf16[2,24,2,512]{3,2,1,0:T(2,128)(2,1)S(1)}, u32[]{:S(2)}, u32[]{:S(2)}) async-start(bf16[2,24,2,512]{3,2,1,0:T(2,128)(2,1)} %broadcast_select_fusion.1), calls=%async_computation | async-start | bytes 196608 | tf_op jit(solution)/shard_map/all_to_all | solution.py:87
  15.2 228.5 %all-reduce.19.cloned.1.call-start = ((), (), s32[]{:S(2)}) async-start(), calls=%async_computation.5 | async-start | bytes 196608 | tf_op jit(solution)/shard_map/psum | solution.py:40
  50.0 0.7 copy-start.14
  51.6 0.7 copy-start.15
  115.8 0.8 copy-start.11
  116.9 0.7 copy-start.2
  118.2 34.1 %copy-start.4 = (bf16[512,256]{1,0:T(8,128)(2,1)S(1)}, bf16[512,256]{1,0:T(8,128)(2,1)}, u32[]{:S(2)}) copy-start(bf16[512,256]{1,0:T(8,128)(2,1)} %param.26) | copy-start | bytes 786436
  170.0 0.7 copy-start.3
  172.3 105.7 %copy-start.6 = (bf16[256,512]{1,0:T(8,128)(2,1)S(1)}, bf16[256,512]{1,0:T(8,128)(2,1)}, u32[]{:S(2)}) copy-start(bf16[256,512]{1,0:T(8,128)(2,1)} %param.28) | copy-start | bytes 786436
  243.7 34.4 %copy-start.8 = (f32[32,256]{1,0:T(8,128)S(1)}, f32[32,256]{1,0:T(8,128)}, u32[]{:S(2)}) copy-start(f32[32,256]{1,0:T(8,128)} %get-tuple-element.64) | copy-start | bytes 98308
  278.0 0.7 copy-start.13
  278.7 0.8 copy-start.9
  279.4 0.8 copy-start.10
  338.2 15.0 %copy-start.5 = (bf16[512,256]{1,0:T(8,128)(2,1)S(1)}, bf16[512,256]{1,0:T(8,128)(2,1)}, u32[]{:S(2)}) copy-start(bf16[512,256]{1,0:T(8,128)(2,1)} %param.29) | copy-start | bytes 786436
  339.1 9.9 %all-to-all-start.1 = ((bf16[16,2,512]{2,1,0:T(2,128)(2,1)}), bf16[16,2,512]{2,1,0:T(2,128)(2,1)S(1)}, u32[]{:S(2)}, u32[]{:S(2)}) async-start(bf16[16,2,512]{2,1,0:T(2,128)(2,1)} %stack.14), calls=%async_computation.1 | async-start | bytes 65536 | tf_op jit(solution)/shard_map/all_to_all | solution.py:132
  349.7 9.9 %all-to-all-start.2 = ((bf16[16,2,512]{2,1,0:T(2,128)(2,1)}), bf16[16,2,512]{2,1,0:T(2,128)(2,1)S(1)}, u32[]{:S(2)}, u32[]{:S(2)}) async-start(bf16[16,2,512]{2,1,0:T(2,128)(2,1)} %stack.16), calls=%async_computation.2 | async-start | bytes 65536 | tf_op jit(solution)/shard_map/all_to_all | solution.py:132
  360.2 9.9 %all-to-all-start.3 = ((bf16[16,2,512]{2,1,0:T(2,128)(2,1)}), bf16[16,2,512]{2,1,0:T(2,128)(2,1)S(1)}, u32[]{:S(2)}, u32[]{:S(2)}) async-start(bf16[16,2,512]{2,1,0:T(2,128)(2,1)} %stack.18), calls=%async_computation.3 | async-start | bytes 65536 | tf_op jit(solution)/shard_map/all_to_all | solution.py:132
  363.7 65.0 %all-reduce.17.cloned.1.call-start = ((), (), s32[]{:S(2)}) async-start(), calls=%async_computation.4 | async-start | bytes 196608 | tf_op jit(solution)/shard_map/psum | solution.py:40
Sparse Core Ops, SparseCore 0:
  170.2 73.4 all-reduce.18
  371.0 57.6 all-reduce.16
